TPU v7x, 128 devices: a whole 4x4x4 slice. The times are simulated.
128 devices in a mesh: seq: 32 (over x, z, core), tp: 4 (over y).
Axes of the slice: x: 4, y: 4, z: 4, core: 2. Of those that a mesh axis runs over, the one named last changes fastest.
Arguments:
- tokens: bfloat16 [8192, 2048], P('seq'), may hold values from -6 to 6
- norm_gain: float32 [2048], replicated, may hold values from 0.1 to 1.9
- qkv_weight: bfloat16 [2048, 4096], P(None, 'tp'), may hold values from -0.125 to 0.125
- conv_weight: float32 [4, 4096], P(None, 'tp'), may hold values from -3 to 3
- gate_down: bfloat16 [2048, 16], replicated, may hold values from -0.125 to 0.125
- gate_up: bfloat16 [16, 1024], P(None, 'tp'), may hold values from -6 to 6
- gate_bias: float32 [1024], P('tp'), may hold values from 0.3 to 8.5
- out_gate_weight: bfloat16 [2048, 2048], P(None, 'tp'), may hold values from -0.125 to 0.125
- head_gain: float32 [512], replicated, may hold values from 0.1 to 1.9
- out_weight: bfloat16 [2048, 2048], P('tp'), may hold values from -0.125 to 0.125
- final_gain: float32 [2048], replicated, may hold values from 0.1 to 1.9
- embedding: bfloat16 [32000, 2048], P(('seq', 'tp')), may hold values from -0.5 to 0.5
- lengths: int32 [8], replicated, may hold values from 1 to 4096, as said below
- packed_order: int32 [8], replicated, may hold values from 0 to 7, each once
Outputs:
- hidden: bfloat16 [8192, 2048], P('seq', 'tp')
- last_states: float32 [8, 4, 256, 512], P(None, 'tp')
- conv_edges: float32 [8, 3, 4096], P(None, None, 'tp')
- last_norms: float32 [8], replicated
- max_logits: float32 [8, 128], P(None, ('seq', 'tp'))
Inputs may be any that keep to these rules, and one draw needn't show every extreme that they name: Request r of the initial order has lengths[r] tokens; the lengths sum to 8192, the largest is 4096 and the smallest is 1 or 2. packed_order names every request once; the packed positions hold the tokens of request packed_order[0], then those of packed_order[1], and so on.
All inputs are finite; a program needn't handle non-finite values.
Results may differ from a plain program's by a relative error of at most 0.015.
Values may be sent and summed in bfloat16 or wider, within the bound.
No kernel may reach another device: no remote copies, remote signals or barrier semaphores. Data moves between devices by JAX's collectives and lax.ppermute only.
A program may use at most 128 MiB of HBM per device.

v0:
```python
from functools import partial
import jax
import jax.numpy as jnp
from jax import lax
from jax.sharding import PartitionSpec as P

DK = 256
DV = 512
KCONV = 4
BLOCK = 64
HIGHEST_PRECISION = lax.Precision.HIGHEST


def prefix(array, axis, combine, identity):
    peers, place = (lax.axis_size(axis), lax.axis_index(axis))
    everything = jax.tree.map(
        lambda part, kind: lax.all_gather(part.astype(kind), axis),
        array,
        (jnp.bfloat16, jnp.bfloat16),
    )
    start = jax.tree.map(
        lambda part, zero: jnp.broadcast_to(jnp.asarray(zero, part.dtype), part.shape),
        array,
        identity,
    )

    def hop(k, before):
        reached = k < place
        new = combine(
            before, jax.tree.map(lambda part, own: part[k].astype(own.dtype), everything, array)
        )
        return jax.tree.map(lambda a, b: jnp.where(reached, a, b), new, before)

    return lax.fori_loop(0, peers, hop, start)


def passed_along(array, axis, by):
    peers = lax.axis_size(axis)
    pairs = [(i, i + by) for i in range(peers) if 0 <= i + by < peers]
    return lax.ppermute(array, axis, pairs)


def segments(lengths, packed_order, positions):
    request_count = lengths.shape[0]
    select = (packed_order[:, None] == jnp.arange(request_count, dtype=jnp.int32)[None, :]).astype(
        jnp.int32
    )
    packed_len = jnp.sum(select * lengths[None, :], axis=1)
    end_points = jnp.cumsum(packed_len)
    starts = end_points - packed_len
    segment = jnp.sum((positions[:, None] >= starts[None, :]).astype(jnp.int32), axis=1) - 1
    last_index = jnp.sum(select * (end_points - 1)[:, None], axis=0)
    return (segment, last_index)


def causal_conv(padded, padded_segment, conv_weight, row_count):
    running = jnp.zeros((row_count, padded.shape[1]), jnp.float32)
    current = padded_segment[KCONV - 1 :]
    for offset in range(KCONV):
        window = padded[offset : offset + row_count]
        same_segment = (padded_segment[offset : offset + row_count] == current)[:, None]
        running = running + jnp.where(same_segment, window, 0.0) * conv_weight[offset]
    return running


def activate(convolved, head_count):
    shaped = convolved.reshape(convolved.shape[0], head_count, 2 * DK + DV)
    channel = jnp.arange(2 * DK + DV)
    return jnp.where(channel < 2 * DK, jax.nn.silu(shaped), shaped).astype(jnp.bfloat16)


def advance(carry_state, key_floats, values, cumulative, segment, segment_before):
    total_decay = cumulative[-1]
    same_tail = (segment == segment[-1])[:, None, None]
    scaled = jnp.where(same_tail, key_floats * jnp.exp(total_decay[None] - cumulative), 0.0).astype(
        jnp.bfloat16
    )
    added = jnp.einsum("jhc,jhv->hcv", scaled, values, preferred_element_type=jnp.float32)
    through = segment[-1] == segment_before
    return jnp.where(through, jnp.exp(total_decay)[:, :, None] * carry_state, 0.0) + added


def state_at_ends(
    end_states, carry_state, key_floats, values, cumulative, segment, segment_before, offset
):
    length = segment.shape[0]
    inside_block = (offset >= 0) & (offset < length)

    def add_ends(previous):
        end_row = jnp.clip(offset, 0, length - 1)
        end_decay = cumulative[end_row]
        end_segment = segment[end_row]
        indices = jnp.arange(length)
        allowed = (
            (indices[None, :] <= end_row[:, None]) & (segment[None, :] == end_segment[:, None])
        )[:, :, None, None]
        spread = jnp.where(allowed, end_decay[:, None] - cumulative[None], 0.0)
        weighted = jnp.where(allowed, key_floats[None] * jnp.exp(spread), 0.0).astype(jnp.bfloat16)
        within = jnp.einsum("rjhc,jhv->rhcv", weighted, values, preferred_element_type=jnp.float32)
        carried = (end_segment == segment_before)[:, None, None, None]
        reached = jnp.where(carried, jnp.exp(end_decay)[:, :, :, None] * carry_state[None], 0.0)
        return jnp.where(inside_block[:, None, None, None], within + reached, previous)

    def keep(previous):
        return previous

    return lax.cond(jnp.any(inside_block), add_ends, keep, end_states)


def block_step(last_index, carry, inputs):
    carry_state, end_states = carry
    queries, key_rows, values, decays, segment, segment_before, block_first = inputs
    cumulative = jnp.cumsum(decays, axis=0)
    length = segment.shape[0]
    indices = jnp.arange(length)
    causal = (indices[None, :] <= indices[:, None]) & (segment[None, :] == segment[:, None])
    allowed = causal[:, :, None, None]
    spread = jnp.where(allowed, cumulative[:, None] - cumulative[None, :], 0.0)
    weights = jnp.where(allowed, jnp.exp(spread), 0.0)
    query_rows = queries.astype(jnp.float32)
    key_floats = key_rows.astype(jnp.float32)
    scores = jnp.sum(query_rows[:, None] * key_floats[None, :] * weights, axis=-1).astype(
        jnp.bfloat16
    )
    inside = jnp.einsum("ijh,jhv->ihv", scores, values, preferred_element_type=jnp.float32)
    carried = (segment == segment_before)[:, None, None]
    outside = jnp.einsum(
        "ihc,hcv->ihv", query_rows * jnp.exp(cumulative), carry_state, precision=HIGHEST_PRECISION
    )
    output = inside + jnp.where(carried, outside, 0.0)
    new_state = advance(carry_state, key_floats, values, cumulative, segment, segment_before)
    end_states = state_at_ends(
        end_states,
        carry_state,
        key_floats,
        values,
        cumulative,
        segment,
        segment_before,
        last_index - block_first,
    )
    return ((new_state, end_states), output)


def state_only(carry_state, inputs):
    block_queries, block_keys, block_values, block_decays, block_segment, before, block_start = (
        inputs
    )
    cumulative = jnp.cumsum(block_decays, axis=0)
    return (
        advance(
            carry_state,
            block_keys.astype(jnp.float32),
            block_values,
            cumulative,
            block_segment,
            before,
        ),
        None,
    )


def head_output(attended, gate_out, head_gain):
    row_count, head_count, value_width = attended.shape
    mean_square = jnp.mean(attended * attended, axis=2, keepdims=True)
    gate_values = jax.nn.silu(
        gate_out.astype(jnp.float32).reshape(row_count, head_count, value_width)
    )
    gated = attended * lax.rsqrt(mean_square + 1e-05) * head_gain * gate_values
    return gated.reshape(row_count, head_count * value_width).astype(jnp.bfloat16)


def carry_in(decay_factor, local_state):

    def combine(earlier, later):
        return (earlier[0] * later[0], later[0][:, :, None] * earlier[1] + later[1])

    identity = (jnp.ones_like(decay_factor), jnp.zeros_like(local_state))
    result = prefix((decay_factor, local_state), "seq", combine, identity)
    return result[1]


def shards(
    tokens,
    norm_gain,
    qkv_weight,
    conv_weight,
    gate_down,
    gate_up,
    gate_bias,
    out_gate_weight,
    head_gain,
    out_weight,
    final_gain,
    embedding,
    lengths,
    packed_order,
):
    row_count = tokens.shape[0]
    head_count = out_weight.shape[0] // DV
    column_count = tokens.shape[1] // lax.axis_size("tp")
    start_row = lax.axis_index("seq") * row_count
    positions = start_row + jnp.arange(-(KCONV - 1), row_count, dtype=jnp.int32)
    segment_all, last_index = segments(lengths, packed_order, positions)
    segment = segment_all[KCONV - 1 :]
    segment_prior = segment_all[KCONV - 2]
    first_index = last_index - lengths + 1
    residual = tokens.astype(jnp.float32)
    normed = (
        residual
        * lax.rsqrt(jnp.mean(residual * residual, axis=1, keepdims=True) + 1e-06)
        * norm_gain
    ).astype(jnp.bfloat16)
    projected = jnp.dot(normed, qkv_weight, preferred_element_type=jnp.float32).astype(jnp.bfloat16)
    rim_rows = passed_along(projected[row_count - (KCONV - 1) :], "seq", 1)
    padded = jnp.concatenate([rim_rows, projected], axis=0)
    convolved = causal_conv(padded.astype(jnp.float32), segment_all, conv_weight, row_count)
    activated = activate(convolved, head_count)
    queries = activated[:, :, :DK]
    key_rows = activated[:, :, DK : 2 * DK]
    values = activated[:, :, 2 * DK :]
    lowrank = jnp.dot(normed, gate_down, preferred_element_type=jnp.float32)
    gate_logits = (
        jnp.dot(lowrank, gate_up.astype(jnp.float32), precision=HIGHEST_PRECISION) + gate_bias
    )
    decays = (jax.nn.log_sigmoid(gate_logits) / 16.0).reshape(row_count, head_count, DK)
    gate_out = jnp.dot(normed, out_gate_weight, preferred_element_type=jnp.float32).astype(
        jnp.bfloat16
    )
    block_count = row_count // BLOCK

    def split_blocks(array):
        return array.reshape((block_count, BLOCK) + array.shape[1:])

    segment_before = segment_all[KCONV - 2 : KCONV - 2 + row_count : BLOCK]
    block_first = start_row + jnp.arange(block_count, dtype=jnp.int32) * BLOCK
    block_inputs = (
        split_blocks(queries),
        split_blocks(key_rows),
        split_blocks(values),
        split_blocks(decays),
        split_blocks(segment),
        segment_before,
        block_first,
    )
    through_shard = segment[-1] == segment_prior
    empty_state = jnp.zeros((head_count, DK, DV), jnp.float32)
    empty_ends = jnp.zeros((lengths.shape[0], head_count, DK, DV), jnp.float32)
    stepper = partial(block_step, last_index)
    local_state, unused_steps = lax.scan(state_only, empty_state, block_inputs)
    decay_factor = jnp.where(through_shard, jnp.exp(jnp.sum(decays, axis=0)), 0.0)
    incoming = carry_in(decay_factor, local_state)
    (unused_state, end_states), attended = lax.scan(stepper, (incoming, empty_ends), block_inputs)
    attended = attended.reshape(row_count, head_count, DV)
    gated = head_output(attended, gate_out, head_gain)
    projected_out = jnp.dot(gated, out_weight, preferred_element_type=jnp.float32)
    summed = lax.psum_scatter(
        projected_out.astype(jnp.bfloat16), "tp", scatter_dimension=1, tiled=True
    ).astype(jnp.float32)
    column_start = lax.axis_index("tp") * column_count
    own_columns = lax.dynamic_slice_in_dim(residual, column_start, column_count, 1)
    hidden = (own_columns + summed).astype(jnp.bfloat16)
    owned_here = (last_index >= start_row) & (last_index < start_row + row_count)
    local_last = jnp.clip(last_index - start_row, 0, row_count - 1)
    last_rows = jnp.where(owned_here[:, None], hidden[local_last].astype(jnp.float32), 0.0)
    edge_list = []
    for offset in range(KCONV - 1):
        located = last_index - (KCONV - 2) + offset
        inside = owned_here & (located >= first_index)
        picked = padded[jnp.clip(located - start_row + KCONV - 1, 0, row_count + KCONV - 2)].astype(
            jnp.float32
        )
        edge_list.append(jnp.where(inside[:, None], picked, 0.0))
    conv_edges = jnp.stack(edge_list, axis=1)
    row_sums, conv_edges, last_states = (
        lax.psum(last_rows.astype(jnp.bfloat16), "seq").astype(jnp.float32),
        lax.psum(conv_edges.astype(jnp.bfloat16), "seq").astype(jnp.float32),
        lax.psum(end_states.astype(jnp.bfloat16), "seq").astype(jnp.float32),
    )
    full_rows = lax.all_gather(row_sums, "tp", axis=1, tiled=True)
    mean_square = jnp.mean(full_rows * full_rows, axis=1)
    last_norms = jnp.sqrt(mean_square)
    final_rows = (full_rows * lax.rsqrt(mean_square[:, None] + 1e-06) * final_gain).astype(
        jnp.bfloat16
    )
    logits = jnp.dot(final_rows, embedding.T, preferred_element_type=jnp.float32)
    max_logits = jnp.max(logits, axis=1, keepdims=True)
    return (hidden, last_states, conv_edges, last_norms, max_logits)


def solution(mesh):
    in_specs = (
        P("seq", None),
        P(),
        P(None, "tp"),
        P(None, "tp"),
        P(),
        P(None, "tp"),
        P("tp"),
        P(None, "tp"),
        P(),
        P("tp", None),
        P(),
        P(("seq", "tp"), None),
        P(),
        P(),
    )
    out_specs = (
        P("seq", "tp"),
        P(None, "tp", None, None),
        P(None, None, "tp"),
        P(),
        P(None, ("seq", "tp")),
    )
    return jax.shard_map(shards, mesh=mesh, in_specs=in_specs, out_specs=out_specs, check_vma=False)
```

profile of v0, /device:TPU:0, one launch (start us, length us, event | category | flops | bytes accessed | tf_op | source)
XLA Modules:
  0.0 477.1 jit_solution(16728195551736005816)
XLA Ops:
  7.2 1.6 multiply_reduce_fusion.1
  9.0 3.9 convolution_convert_fusion.1
  12.9 1.3 collective-permute-start
  14.8 1.7 fusion.70
  21.1 21.8 %while.43 = (s32[]{:T(128)}, f32[1,256,512]{2,1,0:T(8,128)S(1)}, s32[4,64]{1,0:T(4,128)S(1)}, s32[4]{0:T(128)S(1)}, f32[4,64,1,256]{3,2,1,0:T(1,128)}, /*index=5...) while((s32[]{:T(128)}, f32[1,256,512]{2,1,0:T(8,128)S(1)}, ...), condition=%wide.region_7.8_spmd.clone, body=%wide.region_5.7_spmd.clone.sunk | while | flops 18415684 | bytes 1417237 | solution.py:250
  25.3 1.2 fusion.123
  30.8 1.2 fusion.123
  36.2 1.2 fusion.123
  41.7 1.2 fusion.123
  45.5 26.3 %all-gather.2 = bf16[32,1,256]{2,1,0:T(2,128)(2,1)S(1)} all-gather(bf16[1,1,256]{2,1,0:T(2,128)(2,1)S(1)} %reshape.975), channel_id=2, replica_groups=mesh['seq'=32,'tp'=4] {'seq'}, dimensions={0}, use_global_device_ids=true | all-gather | bytes 16896 | tf_op jit(solution)/shard_map/all_gather | solution.py:17
  71.9 29.0 %all-gather.5.cloned.1.call-done = bf16[32,256,512]{2,1,0:T(8,128)(2,1)} async-done(((bf16[1,256,512]{2,1,0:T(8,128)(2,1)}), bf16[32,256,512]{2,1,0:T(8,128)(2,1)}) %all-gather.5.cloned.1.call-update) | async-done | bytes 8388624 | tf_op jit(solution)/shard_map/all_gather | solution.py:17
  101.0 36.2 %while.44 = (s32[]{:T(128)}, f32[1,256,512]{2,1,0:T(8,128)S(1)}, s32[]{:T(128)}, bf16[32,1,256]{2,1,0:T(2,128)(2,1)S(1)}, bf16[32,1,256,512]{3,2,1,0:T(8,128)(2,1)}, /*index=5*/s32[]{:T(128)}, s32[]{:T(128)}) while((s32[]{:T(128)}, f32[1,256,512]{2,1,0:T(8,128)S(1)}, s32[]{:T(128)}, bf16[32,1,256]{2,1,0:T(2,128)(2,1)S(1)}, ...), condition=%wide.region_9.10_spmd.clone, body=%wide.region_8.9_spmd.clone.sunk | while | flops 655620 | bytes 1313385 | solution.py:34
  102.1 1.1 fusion.124
  103.2 1.1 fusion.124
  104.4 1.1 fusion.124
  105.5 1.1 fusion.124
  106.6 1.1 fusion.124
  107.7 1.1 fusion.124
  108.9 1.1 fusion.124
  110.0 1.1 fusion.124
  111.1 1.1 fusion.124
  112.3 1.1 fusion.124
  113.4 1.1 fusion.124
  114.5 1.1 fusion.124
  116.8 1.1 fusion.124
  117.9 1.1 fusion.124
  119.1 1.1 fusion.124
  120.2 1.1 fusion.124
  121.3 1.1 fusion.124
  122.5 1.1 fusion.124
  137.1 1.5 broadcast_in_dim.240
  138.6 54.6 %while.42 = (s32[]{:T(128)}, f32[1,256,512]{2,1,0:T(8,128)S(1)}, bf16[8,1,256,512]{3,2,0,1:T(8,128)(2,1)}, f32[4,64,1,512]{3,1,2,0:T(8,128)}, s32[4,64]{1,0:T(4,...) while((s32[]{:T(128)}, f32[1,256,512]{2,1,0:T(8,128)S(1)}, ...), condition=%wide.region_17.18_spmd, body=%wide.region_11.17_spmd.sunk | while | flops 268659424 | bytes 8804605 | solution.py:253
  144.4 5.7 %conditional.2 = (bf16[8,1,256,512]{3,2,0,1:T(8,128)(2,1)}) conditional(s32[]{:T(128)} %convert_element_type.388, bf16[8,1,256,512]{3,2,0,1:T(8,128)(2,1)} %get-tuple-element.722, (pred[8]{0:T(512)(128)(4,1)S(1)}, s32[8]{0:T(128)S(1)}, s32[64]{0:T(128)S(1)}, bf16[1,64,1,256]{3,2,1,0:T(2,128)(2,1)S(1)}, f32[64,1,256]{2,1,0:T(1,128)S(1)}, ...), branch_computations={%region_14.14_spmd, %region_15.15_spmd} | conditional | flops 139086368 | bytes 5199492 | solution.py:107
  146.4 3.7 fusion
  150.3 2.0 multiply_reduce_fusion.5
  162.5 2.0 multiply_reduce_fusion.5
  174.7 2.0 multiply_reduce_fusion.5
  187.0 2.0 multiply_reduce_fusion.5
  194.5 2.8 fusion.56
  197.3 1.7 convolution_convert_fusion
  199.0 2.8 convert_element_type.287
  203.9 96.7 %all-reduce.3.cloned.1.call-done = bf16[8,1,256,512]{3,2,1,0:T(8,128)(2,1)} async-done(((bf16[8,1,256,512]{3,2,1,0:T(8,128)(2,1)}), bf16[8,1,256,512]{3,2,1,0:T(8,128)(2,1)}) %all-reduce.3.cloned.1.call-update) | async-done | bytes 2097168 | tf_op jit(solution)/shard_map/psum | solution.py:278
  300.6 4.2 convert_element_type.304
  304.8 21.7 %reduce-scatter.2.cloned.1.call-done = bf16[256,512]{1,0:T(8,128)(2,1)} async-done(((bf16[256,2048]{1,0:T(8,128)(2,1)}), bf16[256,512]{1,0:T(8,128)(2,1)}) %reduce-scatter.2.cloned.1.call-update) | async-done | bytes 262160 | tf_op jit(solution)/shard_map/reduce_scatter | solution.py:257
  326.5 1.2 add_convert_fusion
  328.3 126.8 %all-reduce = (bf16[8,3,1024]{2,0,1:T(8,128)(2,1)S(1)}, bf16[8,512]{1,0:T(8,128)(2,1)S(1)}) all-reduce(bf16[8,3,1024]{2,0,1:T(8,128)(2,1)S(1)} %pad_maximum_fusion.1, bf16[8,512]{1,0:T(8,128)(2,1)S(1)} %select_convert_fusion.2), channel_id=1, replica_groups=mesh['seq'=32,'tp'=4] {'seq'}, use_global_device_ids=true, to_apply=%region_21.22 | all-reduce | flops 28672 | bytes 114688 | tf_op jit(solution)/shard_map/psum | solution.py:277
  455.2 11.9 %all_gather.16 = f32[8,2048]{1,0:T(8,128)S(1)} all-gather(f32[8,512]{1,0:T(8,128)S(1)} %convert_element_type.314), channel_id=1, replica_groups=mesh['seq'=32,'tp'=4] {'tp'}, dimensions={1}, use_global_device_ids=true | all-gather | bytes 81920 | tf_op jit(solution)/shard_map/all_gather | solution.py:280
  468.3 2.2 convolution_reduce_fusion
  (259 shorter events, 73.5 us)
Async XLA Ops:
  7.2 190.1 %copy-start = (bf16[512,2048]{1,0:T(8,128)(2,1)S(1)}, bf16[512,2048]{1,0:T(8,128)(2,1)}, u32[]{:S(2)}) copy-start(bf16[512,2048]{1,0:T(8,128)(2,1)} %param.31) | copy-start | bytes 6291460
  7.2 93.8 %all-gather.5.cloned.1.call-start = ((), (), s32[]{:S(2)}) async-start(), calls=%async_computation.3 | async-start | bytes 8650752 | tf_op jit(solution)/shard_map/all_gather | solution.py:17
  8.9 5.3 %copy-start.6 = (s32[8]{0:T(128)S(1)}, s32[8]{0:T(128)}, u32[]{:S(2)}) copy-start(s32[8]{0:T(128)} %param.34) | copy-start | bytes 100
  8.9 5.3 %copy-start.12 = (s32[8]{0:T(128)S(1)}, s32[8]{0:T(128)}, u32[]{:S(2)}) copy-start(s32[8]{0:T(128)} %param.35) | copy-start | bytes 100
  8.9 5.8 %copy-start.4 = (f32[4,1024]{1,0:T(4,128)S(1)}, f32[4,1024]{1,0:T(4,128)}, u32[]{:S(2)}) copy-start(f32[4,1024]{1,0:T(4,128)} %param.25) | copy-start | bytes 49156
  8.9 5.8 %copy-start.7 = (bf16[2048,16]{0,1:T(8,128)(2,1)S(1)}, bf16[2048,16]{0,1:T(8,128)(2,1)}, u32[]{:S(2)}) copy-start(bf16[2048,16]{0,1:T(8,128)(2,1)} %param.26) | copy-start | bytes 196612
  8.9 5.8 %copy-start.9 = (f32[2048]{0:T(1024)S(1)}, f32[2048]{0:T(1024)}, u32[]{:S(2)}) copy-start(f32[2048]{0:T(1024)} %param.23) | copy-start | bytes 24580
  8.9 7.5 %copy-start.8 = (bf16[16,256]{1,0:T(8,128)(2,1)S(1)}, bf16[16,256]{1,0:T(8,128)(2,1)}, u32[]{:S(2)}) copy-start(bf16[16,256]{1,0:T(8,128)(2,1)} %param.27) | copy-start | bytes 24580
  9.0 7.5 %copy-start.11 = (f32[256]{0:T(256)S(1)}, f32[256]{0:T(256)}, u32[]{:S(2)}) copy-start(f32[256]{0:T(256)} %param.28) | copy-start | bytes 3076
  12.9 5.3 %collective-permute-start = (bf16[3,1024]{1,0:T(4,128)(2,1)S(1)}, bf16[3,1024]{1,0:T(4,128)(2,1)S(1)}, u32[]{:S(2)}, u32[]{:S(2)}) collective-permute-start(bf16[3,1024]{1,0:T(4,128)(2,1)S(1)} %slice.111), channel_id=1, source_target_pairs={{0,4},{4,8},{8,12},{12,16},{16,20},{20,24},{24,28},{28,32},{32,36}... | collective-permute-start | bytes 18440 | tf_op jit(solution)/shard_map/ppermute | solution.py:40
  43.6 257.0 %all-reduce.3.cloned.1.call-start = ((), (), s32[]{:S(2)}) async-start(), calls=%async_computation.2 | async-start | bytes 4194304 | tf_op jit(solution)/shard_map/psum | solution.py:278
  193.3 1.0 copy-start.2
  193.3 1.2 copy-start.10
  193.3 133.2 %reduce-scatter.2.cloned.1.call-start = ((), (), s32[]{:S(2)}) async-start(), calls=%async_computation.1 | async-start | bytes 1310720 | tf_op jit(solution)/shard_map/reduce_scatter | solution.py:257
  199.0 2.9 copy-start.1
  203.9 264.4 %copy-start.5 = (f32[2048]{0:T(1024)S(1)}, f32[2048]{0:T(1024)}, u32[]{:S(2)}) copy-start(f32[2048]{0:T(1024)} %param.32) | copy-start | bytes 24580
  327.7 142.9 %copy-start.3 = (bf16[256,512]{1,0:T(8,128)(2,1)}, bf16[256,512]{1,0:T(8,128)(2,1)S(1)}, u32[]{:S(2)}) copy-start(bf16[256,512]{1,0:T(8,128)(2,1)S(1)} %add_convert_fusion) | copy-start | bytes 786436
Sparse Core Ops, SparseCore 0:
  43.7 57.1 all-gather.4
  193.4 107.1 all-reduce.2
  303.0 23.4 reduce-scatter.1
where the time goes:
time: 480 us; the launch traced here: 477 us
  blocking collectives  165 us (34%)
  waiting for transfers between devices  147 us (31%)
  other arithmetic  81.7 us (17%)
  matrix products  27.2 us (6%)
  local copies, waits for them, and re-layouts  24.3 us (5%)
  between operations  15.3 us (3%)
  loops' own time  14.8 us (3%)
    psum x1, blocking collectives, shards(): lax.psum(conv_edges.astype(jnp.bfloat16), 'seq').astype(jnp.float32)  127 us
    psum x1, waiting for transfers between devices, shards(): lax.psum(end_states.astype(jnp.bfloat16), 'seq').astype(jnp.float32)  96.7 us
    select_n x32, other arithmetic, hop(): return jax.tree.map(lambda a, b: jnp.where(reached, a, b), new, before)  34.9 us
    all_gather x1, waiting for transfers between devices, prefix(): lax.all_gather(part.astype(kind), axis)  29 us
    all_gather x1, blocking collectives, prefix(): lax.all_gather(part.astype(kind), axis)  26.3 us
    reduce_scatter x1, waiting for transfers between devices, shards(): lax.psum_scatter(projected_out.astype(jnp.bfloat16), 'tp', scatter_dimens...  21.7 us
    all_gather x1, blocking collectives, shards(): full_rows = lax.all_gather(row_sums, 'tp', axis=1, tiled=True)  11.9 us
    dynamic_slice x24, local copies, waits for them, and re-layouts, shards(): local_state, unused_steps = lax.scan(state_only, empty_state, block_inputs)  10.5 us
  transfers between devices with their start and end apart: 4, of which 3 were waited for; matrix products, arithmetic and copies ran while one was open for 4% of the time, Pallas kernels for 0%

commit v1 on v0

--- a/solution.py
+++ b/solution.py
@@ -1,3 +1,4 @@
+import functools
 from functools import partial
 import jax
 import jax.numpy as jnp
@@ -9,6 +10,13 @@
 KCONV = 4
 BLOCK = 64
 HIGHEST_PRECISION = lax.Precision.HIGHEST
+
+
+def fill_sector_for(body, device_axis):
+    return jnp.sum(lax.all_gather(body, device_axis), axis=0)
+
+
+_draft_array = functools.partial(fill_sector_for, device_axis="seq")
 
 
 def prefix(array, axis, combine, identity):
@@ -274,7 +282,7 @@
     conv_edges = jnp.stack(edge_list, axis=1)
     row_sums, conv_edges, last_states = (
         lax.psum(last_rows.astype(jnp.bfloat16), "seq").astype(jnp.float32),
-        lax.psum(conv_edges.astype(jnp.bfloat16), "seq").astype(jnp.float32),
+        _draft_array(conv_edges.astype(jnp.bfloat16)).astype(jnp.float32),
         lax.psum(end_states.astype(jnp.bfloat16), "seq").astype(jnp.float32),
     )
     full_rows = lax.all_gather(row_sums, "tp", axis=1, tiled=True)

time: 480 us -> 421 us (0.88)
  blocking collectives: 165 us -> 106 us
    psum x1, blocking collectives: 127 us -> 66.8 us  [shards(): lax.psum(last_rows.astype(jnp.bfloat16), 'seq').astype(jnp.float32)]
  transfers between devices with their start and end apart: 4 -> 5, of which waited for: 3 -> 3; matrix products, arithmetic and copies ran while one was open for 4% -> 25% of each run, Pallas kernels for 0% -> 0%
where the time goes in v1:
time: 421 us; the launch traced here: 418 us
  waiting for transfers between devices  144 us (34%)
  blocking collectives  106 us (25%)
  other arithmetic  84.4 us (20%)
  local copies, waits for them, and re-layouts  28 us (7%)
  matrix products  24.5 us (6%)
  between operations  15.4 us (4%)
  loops' own time  14.5 us (3%)
    psum x1, waiting for transfers between devices, shards(): lax.psum(end_states.astype(jnp.bfloat16), 'seq').astype(jnp.float32)  97.6 us
    psum x1, blocking collectives, shards(): lax.psum(last_rows.astype(jnp.bfloat16), 'seq').astype(jnp.float32)  66.8 us
    select_n x32, other arithmetic, hop(): return jax.tree.map(lambda a, b: jnp.where(reached, a, b), new, before)  34.9 us
    all_gather x1, blocking collectives, prefix(): lax.all_gather(part.astype(kind), axis)  27 us
    all_gather x1, waiting for transfers between devices, prefix(): lax.all_gather(part.astype(kind), axis)  25.1 us
    reduce_scatter x1, waiting for transfers between devices, shards(): lax.psum_scatter(projected_out.astype(jnp.bfloat16), 'tp', scatter_dimens...  21.6 us
    dynamic_slice x24, local copies, waits for them, and re-layouts, shards(): local_state, unused_steps = lax.scan(state_only, empty_state, block_inputs)  13.7 us
    all_gather x1, blocking collectives, shards(): full_rows = lax.all_gather(row_sums, 'tp', axis=1, tiled=True)  11.9 us
  transfers between devices with their start and end apart: 5, of which 3 were waited for; matrix products, arithmetic and copies ran while one was open for 25% of the time, Pallas kernels for 0%

profile of v1, /device:TPU:0, one launch (start us, length us, event | category | flops | bytes accessed | tf_op | source)
XLA Modules:
  0.0 418.2 jit_solution(17041458056240697764)
XLA Ops:
  7.2 1.6 multiply_reduce_fusion.1
  9.0 3.9 convolution_convert_fusion.1
  13.7 1.3 collective-permute-start
  17.8 1.2 pad_maximum_fusion
  21.5 21.8 %while.43 = (s32[]{:T(128)}, f32[1,256,512]{2,1,0:T(8,128)S(1)}, s32[4,64]{1,0:T(4,128)S(1)}, s32[4]{0:T(128)S(1)}, f32[4,64,1,256]{3,2,1,0:T(1,128)}, /*index=5...) while((s32[]{:T(128)}, f32[1,256,512]{2,1,0:T(8,128)S(1)}, ...), condition=%wide.region_7.8_spmd.clone, body=%wide.region_5.7_spmd.clone.sunk | while | flops 18415684 | bytes 1417237 | solution.py:258
  25.8 1.2 fusion.126
  31.2 1.2 fusion.126
  36.7 1.2 fusion.126
  42.1 1.2 fusion.126
  46.0 27.0 %all-gather.2 = bf16[32,1,256]{2,1,0:T(2,128)(2,1)S(1)} all-gather(bf16[1,1,256]{2,1,0:T(2,128)(2,1)S(1)} %reshape.1038), channel_id=2, replica_groups=mesh['seq'=32,'tp'=4] {'seq'}, dimensions={0}, use_global_device_ids=true | all-gather | bytes 16896 | tf_op jit(solution)/shard_map/all_gather | solution.py:25
  76.3 25.1 %all-gather.8.cloned.1.call-done = bf16[32,256,512]{2,1,0:T(8,128)(2,1)} async-done(((bf16[1,256,512]{2,1,0:T(8,128)(2,1)}), bf16[32,256,512]{2,1,0:T(8,128)(2,1)}) %all-gather.8.cloned.1.call-update) | async-done | bytes 8388624 | tf_op jit(solution)/shard_map/all_gather | solution.py:25
  101.4 36.2 %while.44 = (s32[]{:T(128)}, f32[1,256,512]{2,1,0:T(8,128)S(1)}, s32[]{:T(128)}, bf16[32,1,256]{2,1,0:T(2,128)(2,1)S(1)}, bf16[32,1,256,512]{3,2,1,0:T(8,128)(2,1)}, /*index=5*/s32[]{:T(128)}, s32[]{:T(128)}) while((s32[]{:T(128)}, f32[1,256,512]{2,1,0:T(8,128)S(1)}, s32[]{:T(128)}, bf16[32,1,256]{2,1,0:T(2,128)(2,1)S(1)}, ...), condition=%wide.region_9.10_spmd.clone, body=%wide.region_8.9_spmd.clone.sunk | while | flops 655620 | bytes 1313385 | solution.py:42
  102.5 1.1 fusion.127
  103.7 1.1 fusion.127
  104.8 1.1 fusion.127
  105.9 1.1 fusion.127
  107.1 1.1 fusion.127
  108.2 1.1 fusion.127
  109.3 1.1 fusion.127
  110.5 1.1 fusion.127
  111.6 1.1 fusion.127
  112.7 1.1 fusion.127
  113.9 1.1 fusion.127
  115.0 1.1 fusion.127
  116.1 1.1 fusion.127
  117.3 1.1 fusion.127
  118.4 1.1 fusion.127
  120.7 1.1 fusion.127
  121.8 1.1 fusion.127
  137.6 1.5 broadcast_in_dim.240
  139.1 57.3 %while.42 = (s32[]{:T(128)}, f32[1,256,512]{2,1,0:T(8,128)S(1)}, bf16[8,1,256,512]{3,2,0,1:T(8,128)(2,1)}, f32[4,64,1,512]{3,1,2,0:T(8,128)}, s32[4,64]{1,0:T(4,...) while((s32[]{:T(128)}, f32[1,256,512]{2,1,0:T(8,128)S(1)}, ...), condition=%wide.region_17.18_spmd, body=%wide.region_11.17_spmd.sunk | while | flops 268659424 | bytes 8804605 | solution.py:261
  145.6 5.7 %conditional.2 = (bf16[8,1,256,512]{3,2,0,1:T(8,128)(2,1)}) conditional(s32[]{:T(128)} %convert_element_type.415, bf16[8,1,256,512]{3,2,0,1:T(8,128)(2,1)} %get-tuple-element.720, (pred[8]{0:T(512)(128)(4,1)S(1)}, s32[8]{0:T(128)S(1)}, s32[64]{0:T(128)S(1)}, bf16[1,64,1,256]{3,2,1,0:T(2,128)(2,1)S(1)}, f32[64,1,256]{2,1,0:T(1,128)S(1)}, ...), branch_computations={%region_14.14_spmd, %region_15.15_spmd} | conditional | flops 139086368 | bytes 5199492 | solution.py:115
  147.6 3.7 fusion
  151.5 2.0 multiply_reduce_fusion.5
  164.4 2.0 multiply_reduce_fusion.5
  177.3 2.0 multiply_reduce_fusion.5
  190.2 2.0 multiply_reduce_fusion.5
  196.5 1.2 multiply_reduce_fusion.2
  197.9 2.5 fusion.56
  200.4 1.7 convolution_convert_fusion
  202.2 1.5 convert_element_type.314
  203.7 1.7 reduce_sum.90
  206.1 97.6 %all-reduce.2.cloned.1.call-done = bf16[8,1,256,512]{3,2,1,0:T(8,128)(2,1)} async-done(((bf16[8,1,256,512]{3,2,1,0:T(8,128)(2,1)}), bf16[8,1,256,512]{3,2,1,0:T(8,128)(2,1)}) %all-reduce.2.cloned.1.call-update) | async-done | bytes 2097168 | tf_op jit(solution)/shard_map/psum | solution.py:286
  303.8 4.2 convert_element_type.331
  307.9 21.6 %reduce-scatter.2.cloned.1.call-done = bf16[256,512]{1,0:T(8,128)(2,1)} async-done(((bf16[256,2048]{1,0:T(8,128)(2,1)}), bf16[256,512]{1,0:T(8,128)(2,1)}) %reduce-scatter.2.cloned.1.call-update) | async-done | bytes 262160 | tf_op jit(solution)/shard_map/reduce_scatter | solution.py:265
  329.5 1.2 add_convert_fusion
  331.4 66.8 %psum.15 = bf16[8,512]{1,0:T(8,128)(2,1)S(1)} all-reduce(bf16[8,512]{1,0:T(8,128)(2,1)S(1)} %select_convert_fusion.2), channel_id=1, replica_groups=mesh['seq'=32,'tp'=4] {'seq'}, use_global_device_ids=true, to_apply=%region_22.23 | all-reduce | flops 4096 | bytes 16384 | tf_op jit(solution)/shard_map/psum | solution.py:284
  398.1 11.9 %all_gather.21 = f32[8,2048]{1,0:T(8,128)S(1)} all-gather(f32[8,512]{1,0:T(8,128)S(1)} %convert_element_type.341), channel_id=1, replica_groups=mesh['seq'=32,'tp'=4] {'tp'}, dimensions={1}, use_global_device_ids=true | all-gather | bytes 81920 | tf_op jit(solution)/shard_map/all_gather | solution.py:288
  (273 shorter events, 79.6 us)
Async XLA Ops:
  7.2 193.2 %copy-start = (bf16[512,2048]{1,0:T(8,128)(2,1)S(1)}, bf16[512,2048]{1,0:T(8,128)(2,1)}, u32[]{:S(2)}) copy-start(bf16[512,2048]{1,0:T(8,128)(2,1)} %param.31) | copy-start | bytes 6291460
  7.2 94.2 %all-gather.8.cloned.1.call-start = ((), (), s32[]{:S(2)}) async-start(), calls=%async_computation.4 | async-start | bytes 8650752 | tf_op jit(solution)/shard_map/all_gather | solution.py:25
  8.9 6.1 %copy-start.8 = (s32[8]{0:T(128)S(1)}, s32[8]{0:T(128)}, u32[]{:S(2)}) copy-start(s32[8]{0:T(128)} %param.34) | copy-start | bytes 100
  8.9 6.1 %copy-start.14 = (s32[8]{0:T(128)S(1)}, s32[8]{0:T(128)}, u32[]{:S(2)}) copy-start(s32[8]{0:T(128)} %param.35) | copy-start | bytes 100
  8.9 6.7 %copy-start.6 = (f32[4,1024]{1,0:T(4,128)S(1)}, f32[4,1024]{1,0:T(4,128)}, u32[]{:S(2)}) copy-start(f32[4,1024]{1,0:T(4,128)} %param.25) | copy-start | bytes 49156
  8.9 6.7 %copy-start.1 = (bf16[256,2048]{1,0:T(8,128)(2,1)S(1)}, bf16[256,2048]{1,0:T(8,128)(2,1)}, u32[]{:S(2)}) copy-start(bf16[256,2048]{1,0:T(8,128)(2,1)} %param.22) | copy-start | bytes 3145732
  8.9 6.7 %copy-start.9 = (bf16[2048,16]{0,1:T(8,128)(2,1)S(1)}, bf16[2048,16]{0,1:T(8,128)(2,1)}, u32[]{:S(2)}) copy-start(bf16[2048,16]{0,1:T(8,128)(2,1)} %param.26) | copy-start | bytes 196612
  8.9 6.7 %copy-start.11 = (f32[2048]{0:T(1024)S(1)}, f32[2048]{0:T(1024)}, u32[]{:S(2)}) copy-start(f32[2048]{0:T(1024)} %param.23) | copy-start | bytes 24580
  9.0 7.1 %copy-start.10 = (bf16[16,256]{1,0:T(8,128)(2,1)S(1)}, bf16[16,256]{1,0:T(8,128)(2,1)}, u32[]{:S(2)}) copy-start(bf16[16,256]{1,0:T(8,128)(2,1)} %param.27) | copy-start | bytes 24580
  9.0 7.1 %copy-start.13 = (f32[256]{0:T(256)S(1)}, f32[256]{0:T(256)}, u32[]{:S(2)}) copy-start(f32[256]{0:T(256)} %param.28) | copy-start | bytes 3076
  12.9 0.8 copy-start.4
  13.7 4.1 collective-permute-start
  43.3 30.3 %copy-start.15 = (s32[4]{0:T(128)}, s32[4]{0:T(128)S(1)}, u32[]{:S(2)}) copy-start(s32[4]{0:T(128)S(1)} %get-tuple-element.765) | copy-start | bytes 52
  44.1 159.6 %all-gather.6.cloned.1.call-start = ((), (), s32[]{:S(2)}) async-start(), calls=%async_computation.3 | async-start | bytes 1622016 | tf_op jit(solution)/shard_map/all_gather | solution.py:16
  76.3 227.5 %all-reduce.2.cloned.1.call-start = ((), (), s32[]{:S(2)}) async-start(), calls=%async_computation.2 | async-start | bytes 4194304 | tf_op jit(solution)/shard_map/psum | solution.py:286
  137.6 1.5 copy-start.16
  137.6 1.5 copy-start.17
  196.4 1.4 copy-start.2
  196.5 1.4 copy-start.12
  196.5 133.0 %reduce-scatter.2.cloned.1.call-start = ((), (), s32[]{:S(2)}) async-start(), calls=%async_computation.1 | async-start | bytes 1310720 | tf_op jit(solution)/shard_map/reduce_scatter | solution.py:265
  206.1 204.5 %copy-start.3 = (bf16[250,2048]{1,0:T(8,128)(2,1)S(1)}, bf16[250,2048]{1,0:T(8,128)(2,1)}, u32[]{:S(2)}) copy-start(bf16[250,2048]{1,0:T(8,128)(2,1)} %param.33) | copy-start | bytes 3072004
  206.1 204.5 %copy-start.7 = (f32[2048]{0:T(1024)S(1)}, f32[2048]{0:T(1024)}, u32[]{:S(2)}) copy-start(f32[2048]{0:T(1024)} %param.32) | copy-start | bytes 24580
  330.7 81.0 %copy-start.5 = (bf16[256,512]{1,0:T(8,128)(2,1)}, bf16[256,512]{1,0:T(8,128)(2,1)S(1)}, u32[]{:S(2)}) copy-start(bf16[256,512]{1,0:T(8,128)(2,1)S(1)} %add_convert_fusion) | copy-start | bytes 786436
Sparse Core Ops, SparseCore 0:
  44.2 57.1 all-gather.7
  104.2 42.5 all-gather.5
  196.6 107.0 all-reduce.1
  306.0 23.4 reduce-scatter.1
